TPU v7x, 256 devices: a whole 4x4x8 slice. The times are simulated.
256 devices in a mesh: facet: 8 (over y_lo, x), vis: 16 (over z, core), spec: 2 (over y_hi).
Axes of the slice: x: 4, y: 4 (y_hi: 2, y_lo: 2; y = y_hi * 2 + y_lo), z: 8, core: 2. Of those that a mesh axis runs over, the one named last changes fastest.
Arguments:
- image: float32 [1024, 8, 4096], P(('facet', 'vis'), 'spec'), may hold values from 0 to 1
- wavelet_dual: float32 [1024, 8, 4096], P(('facet', 'vis'), 'spec'), may hold values from -6 to 6
- weights: float32 [1024, 4096], P(('facet', 'vis')), may hold values from 0.3 to 3
- kernels: bfloat16 [8, 16, 2, 256, 128], P('facet', 'vis'), may hold values from -0.375 to 0.375
- vis_data: bfloat16 [8, 16, 8, 2, 16, 256, 128], P('facet', 'vis', 'spec'), may hold values from -6 to 6
- tile_list: int32 [8, 16, 16], P('facet', 'vis'), may hold values from 0 to 31, as said below
- tile_count: int32 [8, 16], P('facet', 'vis'), may hold values from 4 to 16, as said below
Outputs:
- image_next: float32 [1024, 8, 4096], P(('facet', 'vis'), 'spec')
- dual_next: float32 [1024, 8, 4096], P(('facet', 'vis'), 'spec')
Inputs may be any that keep to these rules, and one draw needn't show every extreme that they name: `tile_list`: the 16 slots of a block name distinct tiles; slots from tile_count on are unused. `tile_count`: every draw has a block with 16 occupied slots and one with the fewest allowed.
All inputs are finite; a program needn't handle non-finite values.
Results may differ from a plain program's by a relative error of at most 0.017.
Values may be sent and summed in bfloat16 or wider, within the bound.
No kernel may reach another device: no remote copies, remote signals or barrier semaphores. Data moves between devices by JAX's collectives and lax.ppermute only.
A program may use at most 128 MiB of HBM per device.

v0:
```python
import math
import jax
import jax.numpy as jnp
from jax import lax
from jax.sharding import PartitionSpec as P

root_three = math.sqrt(3.0)
norm_factor = 4.0 * math.sqrt(2.0)
low_taps = [
    (1.0 + root_three) / norm_factor,
    (3.0 + root_three) / norm_factor,
    (3.0 - root_three) / norm_factor,
    (1.0 - root_three) / norm_factor,
]
high_taps = [low_taps[3], -low_taps[2], low_taps[1], -low_taps[0]]
primal_step = 0.2
dual_step = 0.5
tile_width = 128
highest = lax.Precision.HIGHEST


def shifted(value, axis, steps):
    count = lax.axis_size(axis)
    initial, last = (max(0, -steps), min(count, count - steps))
    return lax.ppermute(value, axis, [(source, source + steps) for source in range(initial, last)])


def for_sending(x):

    def short(part):
        return part.astype(jnp.bfloat16) if part.dtype == jnp.float32 else part

    return jax.tree.map(short, x)


def phase_table(rows_count, cols_count, modulus):
    rows_index = jnp.arange(rows_count, dtype=jnp.int32)
    cols_index = jnp.arange(cols_count, dtype=jnp.int32)
    angle = (rows_index[:, None] * cols_index[None, :] % modulus).astype(jnp.float32) * (
        2.0 * math.pi / modulus
    )
    return (jnp.cos(angle), jnp.sin(angle))


def across_outer(values, table):
    return jnp.einsum(
        "qab,ak->qkb", values, table, precision=highest, preferred_element_type=jnp.float32
    )


def along_inner(values, table):
    return jnp.einsum(
        "qkb,bj->qkj", values, table, precision=highest, preferred_element_type=jnp.float32
    )


def fourier_rows(real_part, imag_part, sign):
    rows_count, length = real_part.shape
    outer = length // tile_width
    cos_outer, sin_outer = phase_table(outer, outer, outer)
    cos_twist, sin_twist = phase_table(outer, tile_width, length)
    cos_inner, sin_inner = phase_table(tile_width, tile_width, tile_width)
    first_re = real_part.reshape(rows_count, outer, tile_width)
    first_im = imag_part.reshape(rows_count, outer, tile_width)
    section_re = across_outer(first_re, cos_outer) - sign * across_outer(first_im, sin_outer)
    section_im = across_outer(first_im, cos_outer) + sign * across_outer(first_re, sin_outer)
    twist_re = section_re * cos_twist - sign * section_im * sin_twist
    twist_im = section_im * cos_twist + sign * section_re * sin_twist
    final_re = along_inner(twist_re, cos_inner) - sign * along_inner(twist_im, sin_inner)
    final_im = along_inner(twist_im, cos_inner) + sign * along_inner(twist_re, sin_inner)
    unit_scale = 1.0 / math.sqrt(length)
    final_re = jnp.swapaxes(final_re, 1, 2).reshape(rows_count, length) * unit_scale
    final_im = jnp.swapaxes(final_im, 1, 2).reshape(rows_count, length) * unit_scale
    return (final_re, final_im)


def kernel_blocks(kernel_pair):
    real_k = kernel_pair[0]
    imag_k = kernel_pair[1]
    top_row = jnp.stack([real_k, -imag_k], axis=1)
    bottom_row = jnp.stack([imag_k, real_k], axis=1)
    return jnp.stack([top_row, bottom_row], axis=0)


def per_device(image, wavelet_dual, weights, kernels, vis_data, tile_list, tile_count):
    panel_rows, chan_count, grid_width = image.shape
    tiles_count = grid_width // tile_width
    stacked = kernel_blocks(kernels[0, 0])
    own_list = tile_list[0, 0]
    slots_count = own_list.shape[0]
    own_data = vis_data[0, 0]
    own_count = tile_count[0, 0]
    columns = jnp.arange(tiles_count, dtype=jnp.int32)
    one_hot = (own_list[:, None] == columns[None, :]).astype(jnp.bfloat16)
    image_rows = image.reshape(panel_rows * chan_count, grid_width)
    grid_re, grid_im = fourier_rows(image_rows, jnp.zeros_like(image_rows), -1.0)
    grid_panel = (
        jnp.stack([grid_re, grid_im], axis=1)
        .reshape(panel_rows, chan_count, 2, grid_width)
        .astype(jnp.bfloat16)
    )
    live_slots = (jnp.arange(slots_count, dtype=jnp.int32) < own_count)[None, None, :, None, None]
    shard_rows = lax.all_gather(grid_panel, "vis", axis=0, tiled=True)
    rows_here = shard_rows.shape[0]
    split_rows = shard_rows.reshape(rows_here, chan_count, 2, tiles_count, tile_width)
    picked = jnp.einsum(
        "rcitn,kt->rcikn", split_rows, one_hot, preferred_element_type=jnp.float32
    ).astype(jnp.bfloat16)
    kernel_rows = stacked
    predicted = jnp.einsum(
        "omir,rcikn->cokmn", kernel_rows, picked, preferred_element_type=jnp.float32
    )
    residual = jnp.where(live_slots, predicted - own_data.astype(jnp.float32), 0.0).astype(
        jnp.bfloat16
    )
    kernel_rows = stacked
    partial_tiles = jnp.einsum(
        "omir,cokmn->rcikn", kernel_rows, residual, preferred_element_type=jnp.float32
    ).astype(jnp.bfloat16)
    placed = jnp.einsum(
        "rcikn,kt->rcitn", partial_tiles, one_hot, preferred_element_type=jnp.float32
    )
    grid_sums = lax.psum_scatter(
        placed.reshape(lax.axis_size("vis") * panel_rows, chan_count, 2, grid_width).astype(
            jnp.bfloat16
        ),
        "vis",
        scatter_dimension=0,
        tiled=True,
    ).astype(jnp.float32)
    sums_rows = grid_sums.reshape(panel_rows * chan_count, 2, grid_width)
    grad_re, grad_im = fourier_rows(sums_rows[:, 0], sums_rows[:, 1], 1.0)
    gradient = grad_re.reshape(panel_rows, chan_count, grid_width)
    upper_rim = shifted(
        wavelet_dual[panel_rows - 3 :].astype(jnp.bfloat16), ("facet", "vis"), 1
    ).astype(jnp.float32)
    padded_dual = jnp.concatenate([upper_rim, wavelet_dual], axis=0)
    synthesized = jnp.zeros_like(wavelet_dual)
    for offset in range(4):
        synthesized = (
            synthesized + high_taps[offset] * padded_dual[3 - offset : 3 - offset + panel_rows]
        )
    image_next = jnp.maximum(image - primal_step * (gradient + synthesized), 0.0)
    extrap = 2.0 * image_next - image
    lower_rim = shifted(for_sending(extrap[:3]), ("facet", "vis"), -1)
    padded_next = jnp.concatenate([extrap, lower_rim], axis=0)
    detail = jnp.zeros_like(extrap)
    for offset in range(4):
        detail = detail + high_taps[offset] * padded_next[offset : offset + panel_rows]
    update = wavelet_dual + dual_step * detail
    energy = lax.psum(jnp.sum(update * update, axis=1).astype(jnp.bfloat16), "spec").astype(
        jnp.float32
    )
    dual_next = update * weights[:, None, :] / jnp.maximum(weights, jnp.sqrt(energy))[:, None, :]
    return (image_next, dual_next)


def solution(mesh):
    return jax.shard_map(
        per_device,
        mesh=mesh,
        in_specs=(
            P(("facet", "vis"), "spec", None),
            P(("facet", "vis"), "spec", None),
            P(("facet", "vis"), None),
            P("facet", "vis", None, None, None),
            P("facet", "vis", "spec", None, None, None, None),
            P("facet", "vis", None),
            P("facet", "vis"),
        ),
        out_specs=(P(("facet", "vis"), "spec", None), P(("facet", "vis"), "spec", None)),
        check_vma=False,
    )
```

profile of v0, /device:TPU:1, one launch (start us, length us, event | category | flops | bytes accessed | tf_op | source)
XLA Modules:
  0.0 359.4 jit_solution(1260190742002572805)
XLA Ops:
  7.3 0.4 fusion.58
  7.7 1.4 reshape_reshape.3
  9.1 0.7 fusion.97
  9.8 0.4 fusion.20
  10.2 0.8 subtract_bitcast_fusion.1
  11.0 1.1 fusion.54
  12.1 1.1 fusion.50
  13.2 1.1 fusion.24
  14.3 0.5 copy.63
  14.8 1.0 mul.458
  15.8 1.1 fusion.23
  16.9 0.5 copy.66
  17.5 1.0 mul.462
  18.5 1.2 pad_maximum_fusion.2
  19.7 0.2 all-reduce.6.cloned.1.call-start
  19.9 11.5 %copy.69 = bf16[1,1,4,2,16,256,128]{5,6,4,3,2,1,0:T(8,128)(2,1)} copy(bf16[1,1,4,2,16,256,128]{6,5,4,3,2,1,0:T(8,128)(2,1)} %param.11) | data formatting | bytes 16777216 | tf_op args[4]
  32.1 47.8 %all-gather.2.cloned.1.call-done = bf16[128,4,2,4096]{3,1,0,2:T(4,128)(2,1)} async-done(((bf16[8,4,2,4096]{3,1,0,2:T(4,128)(2,1)}), bf16[128,4,2,4096]{3,1,0,2:T(4,128)(2,1)}) %all-gather.2.cloned.1.call-update) | async-done | bytes 8388624 | tf_op jit(solution)/shard_map/all_gather | solution.py:103
  80.0 15.8 %reshape.128 = bf16[128,4,2,32,128]{4,3,1,0,2:T(8,128)(2,1)} reshape(bf16[128,4,2,4096]{3,1,0,2:T(4,128)(2,1)} %all-gather.2.cloned.1.call-done) | data formatting | bytes 16777216 | tf_op jit(solution)/shard_map/reshape | solution.py:105
  95.7 4.7 %convert_bitcast_fusion.1 = bf16[128,4,2,16,128,1]{4,3,2,1,0,5:T(8,128)(2,1)S(1)} fusion(bf16[128,4,2,32,128]{4,3,1,0,2:T(8,128)(2,1)} %reshape.128, s32[16]{0:T(128)S(1)} %bitcast.129), kind=kOutput, calls=%fused_computation.12 | convolution fusion | flops 136315392 | bytes 12582976 | tf_op jit(solution)/shard_map/rcitn,kt->rcikn/dot_general | solution.py:106
  100.4 15.2 %fusion.6 = bf16[4,2,16,256,128,1]{3,4,2,1,0,5:T(8,128)(2,1)} fusion(bf16[1,1,4,2,16,256,128]{5,6,4,3,2,1,0:T(8,128)(2,1)} %copy.69, pred[16]{0:T(512)(128)(4,1)S(1)} %iota_compare_fusion.1, bf16[128,4,2,16,128,1]{4,3,2,1,0,5:T(8,128)(2,1)S(1)} %convert_bitcast_fusion.1, bf16[1,256,2,128]{3,1,2,0:T(8,128)(2,1)S(1)} %get-tuple-element.15, ...), kind=kOutput, calls=%fused_computation.9 | convolution fusion | flops 2164785152 | bytes 21233680 | tf_op jit(solution)/shard_map/omir,rcikn->cokmn/dot_general | solution.py:110
  115.7 7.7 %fusion.7 = bf16[128,4,2,16,128]{0,4,2,3,1:T(8,128)(2,1)} fusion(bf16[4,2,16,256,128,1]{3,4,2,1,0,5:T(8,128)(2,1)} %fusion.6, bf16[1,256,2,128]{3,1,2,0:T(8,128)(2,1)S(1)} %get-tuple-element.15, bf16[1,256,2,128]{3,1,2,0:T(8,128)(2,1)S(1)} %get-tuple-element.14), kind=kOutput, calls=%fused_computation.10 | convolution fusion | flops 2149711872 | bytes 12845056 | tf_op jit(solution)/shard_map/omir,cokmn->rcikn/dot_general | solution.py:117
  123.4 8.0 %copy.72 = bf16[128,4,2,16,128]{4,3,2,1,0:T(8,128)(2,1)} copy(bf16[128,4,2,16,128]{0,4,2,3,1:T(8,128)(2,1)} %fusion.7) | data formatting | bytes 8388608 | tf_op jit(solution)/shard_map/convert_element_type | solution.py:119
  131.3 7.8 %convert_bitcast_fusion = bf16[128,4,2,32,128]{4,3,2,1,0:T(8,128)(2,1)} fusion(bf16[128,4,2,16,128]{4,3,2,1,0:T(8,128)(2,1)} %copy.72, s32[16]{0:T(128)S(1)} %bitcast.130), kind=kOutput, calls=%fused_computation.8 | convolution fusion | flops 138412544 | bytes 12582976 | tf_op jit(solution)/shard_map/rcikn,kt->rcitn/dot_general | solution.py:120
  139.2 12.5 %convert_element_type.116 = bf16[128,4,2,4096]{3,2,1,0:T(2,128)(2,1)} reshape(bf16[128,4,2,32,128]{4,3,2,1,0:T(8,128)(2,1)} %convert_bitcast_fusion) | data formatting | bytes 16777216 | tf_op jit(solution)/shard_map/convert_element_type | solution.py:124
  151.7 11.0 %copy.73 = bf16[128,4,2,4096]{3,1,2,0:T(4,128)(2,1)} copy(bf16[128,4,2,4096]{3,2,1,0:T(2,128)(2,1)} %convert_element_type.116) | data formatting | bytes 16777216 | tf_op jit(solution)/shard_map/convert_element_type | solution.py:124
  162.8 1.0 copy-done
  163.8 1.9 collective-permute-start
  165.7 0.6 dynamic-slice
  167.1 0.3 collective-permute-done
  167.4 127.4 %all-reduce.6.cloned.1.call-done = bf16[128,4,2,4096]{3,1,2,0:T(4,128)(2,1)} async-done(((bf16[128,4,2,4096]{3,1,2,0:T(4,128)(2,1)}), bf16[128,4,2,4096]{3,1,2,0:T(4,128)(2,1)}) %all-reduce.6.cloned.1.call-update) | async-done | bytes 8388624
  294.7 1.2 constant_dynamic-slice_fusion
  296.0 0.5 copy.74
  296.5 2.3 slice_reduce_fusion.1
  298.8 0.4 fusion.92
  299.3 0.4 fusion.94
  299.8 0.4 convolution_add_fusion
  300.2 0.6 add_bitcast_fusion
  300.8 1.1 fusion.47
  301.9 1.1 fusion.14
  303.0 0.6 copy.77
  303.6 0.9 mul.470
  304.6 2.4 multiply_subtract_fusion
  307.0 4.0 %collective-permute-start.1 = (bf16[3,4,4096]{2,1,0:T(4,128)(2,1)S(1)}, bf16[3,4,4096]{2,1,0:T(4,128)(2,1)S(1)}, u32[]{:S(2)}, u32[]{:S(2)}) collective-permute-start(bf16[3,4,4096]{2,1,0:T(4,128)(2,1)S(1)} %slice.138), channel_id=1, source_target_pairs={{2,0},{4,2},{6,4},{8,6},{10,8},{12,10},{14,12},{16,14},{18,16},{20... | collective-permute-start | bytes 294920 | tf_op jit(solution)/shard_map/ppermute | solution.py:25
  311.0 1.9 collective-permute-done.1
  313.0 1.3 multiply_reduce_fusion
  314.3 36.7 %all-reduce.4.cloned.1.call-done = bf16[8,4096]{1,0:T(8,128)(2,1)} async-done(((bf16[8,4096]{1,0:T(8,128)(2,1)}), bf16[8,4096]{1,0:T(8,128)(2,1)}) %all-reduce.4.cloned.1.call-update) | async-done | bytes 65552 | tf_op jit(solution)/shard_map/psum | solution.py:151
  351.1 0.9 sqrt_maximum_fusion
  351.9 1.0 multiply_divide_fusion
  (26 shorter events, 0.6 us)
Async XLA Ops:
  7.2 72.8 %all-gather.2.cloned.1.call-start = ((), (), s32[]{:S(2)}) async-start(), calls=%async_computation | async-start | bytes 8912896 | tf_op jit(solution)/shard_map/all_gather | solution.py:103
  19.7 12.4 %copy-start.2 = (bf16[1,1,2,256,128]{4,3,2,1,0:T(8,128)(2,1)S(1)}, bf16[1,1,2,256,128]{4,3,2,1,0:T(8,128)(2,1)}, u32[]{:S(2)}) copy-start(bf16[1,1,2,256,128]{4,3,2,1,0:T(8,128)(2,1)} %param.10) | copy-start | bytes 393220
  19.7 275.0 %all-reduce.6.cloned.1.call-start = ((), (), s32[]{:S(2)}) async-start(), calls=%async_computation.2 | async-start | bytes 16777216
  32.1 63.6 %copy-start.3 = (s32[1,1,16]{2,1,0:T(1,128)S(1)}, s32[1,1,16]{2,1,0:T(1,128)}, u32[]{:S(2)}) copy-start(s32[1,1,16]{2,1,0:T(1,128)} %param.12) | copy-start | bytes 196
  162.7 1.0 copy-start
  162.7 3.0 copy-start.4
  162.8 188.3 %all-reduce.4.cloned.1.call-start = ((), (), s32[]{:S(2)}) async-start(), calls=%async_computation.1 | async-start | bytes 131072 | tf_op jit(solution)/shard_map/psum | solution.py:151
  163.8 3.5 collective-permute-start
  299.8 51.3 %copy-start.1 = (f32[8,4096]{1,0:T(8,128)S(1)}, f32[8,4096]{1,0:T(8,128)}, u32[]{:S(2)}) copy-start(f32[8,4096]{1,0:T(8,128)} %param.9) | copy-start | bytes 393220
  307.0 5.9 %collective-permute-start.1 = (bf16[3,4,4096]{2,1,0:T(4,128)(2,1)S(1)}, bf16[3,4,4096]{2,1,0:T(4,128)(2,1)S(1)}, u32[]{:S(2)}, u32[]{:S(2)}) collective-permute-start(bf16[3,4,4096]{2,1,0:T(4,128)(2,1)S(1)} %slice.138), channel_id=1, source_target_pairs={{2,0},{4,2},{6,4},{8,6},{10,8},{12,10},{14,12},{16,14},{18,16},{20... | collective-permute-start | bytes 294920 | tf_op jit(solution)/shard_map/ppermute | solution.py:25
Sparse Core Ops, SparseCore 0:
  19.8 60.1 all-gather.1
  162.9 131.8 all-reduce.5
  314.4 36.5 all-reduce.3
where the time goes:
time: 361 us; the launch traced here: 359 us
  waiting for transfers between devices  214 us (59%)
  local copies, waits for them, and re-layouts  70.6 us (20%)
  matrix products  46.1 us (13%)
  between operations  15.3 us (4%)
  other arithmetic  7.01 us (2%)
  starting transfers between devices  6.25 us (2%)
    unnamed x4, waiting for transfers between devices  127 us
    all_gather x1, waiting for transfers between devices, per_device(): shard_rows = lax.all_gather(grid_panel, 'vis', axis=0, tiled=True)  47.8 us
    psum x1, waiting for transfers between devices, per_device(): lax.psum(jnp.sum(update * update, axis=1).astype(jnp.bfloat16), 'spec')  36.7 us
    convert_element_type x2, local copies, waits for them, and re-layouts, per_device(): placed.reshape(lax.axis_size('vis') * panel_rows, chan_count, 2, grid_width)  23.6 us
    reshape x1, local copies, waits for them, and re-layouts, per_device(): shard_rows.reshape(rows_here, chan_count, 2, tiles_count, tile_width)  15.8 us
    dot_general x1, matrix products, per_device(): jnp.einsum('omir,rcikn->cokmn', kernel_rows, picked, preferred_element_ty...  15.2 us
    unnamed x15, local copies, waits for them, and re-layouts  14.3 us
    convert_element_type x1, local copies, waits for them, and re-layouts, per_device(): partial_tiles = jnp.einsum('omir,cokmn->rcikn', kernel_rows, residual, pr...  7.97 us
  transfers between devices with their start and end apart: 5, of which 5 were waited for; matrix products, arithmetic and copies ran while one was open for 3% of the time, Pallas kernels for 0%

commit v1 on v0

--- a/solution.py
+++ b/solution.py
@@ -148,9 +148,9 @@
     for offset in range(4):
         detail = detail + high_taps[offset] * padded_next[offset : offset + panel_rows]
     update = wavelet_dual + dual_step * detail
-    energy = lax.psum(jnp.sum(update * update, axis=1).astype(jnp.bfloat16), "spec").astype(
-        jnp.float32
-    )
+    energy = jnp.sum(
+        lax.all_gather(jnp.sum(update * update, axis=1).astype(jnp.bfloat16), "spec"), axis=0
+    ).astype(jnp.float32)
     dual_next = update * weights[:, None, :] / jnp.maximum(weights, jnp.sqrt(energy))[:, None, :]
     return (image_next, dual_next)
 

time: 361 us -> 332 us (0.920)
  waiting for transfers between devices: 214 us -> 177 us
  blocking collectives: 0 us -> 5.98 us
    psum x1 -> x0, waiting for transfers between devices: 36.7 us -> none  [per_device(): lax.psum(jnp.sum(update * update, axis=1).astype(jnp.bfloat16), 'spec')]
    all_gather x0 -> x1, blocking collectives: none -> 5.98 us  [per_device(): lax.all_gather(jnp.sum(update * update, axis=1).astype(jnp.bfloat16), 'sp...]
    unnamed x4 -> x3, waiting for transfers between devices: 127 us -> 127 us
  transfers between devices with their start and end apart: 5 -> 4, of which waited for: 5 -> 4; matrix products, arithmetic and copies ran while one was open for 3% -> 4% of each run, Pallas kernels for 0% -> 0%
where the time goes in v1:
time: 332 us; the launch traced here: 328 us
  waiting for transfers between devices  177 us (53%)
  local copies, waits for them, and re-layouts  70.7 us (21%)
  matrix products  46 us (14%)
  between operations  15.6 us (5%)
  starting transfers between devices  6.21 us (2%)
  blocking collectives  5.98 us (2%)
  other arithmetic  5.59 us (2%)
    unnamed x3, waiting for transfers between devices  127 us
    all_gather x1, waiting for transfers between devices, per_device(): shard_rows = lax.all_gather(grid_panel, 'vis', axis=0, tiled=True)  47.8 us
    convert_element_type x2, local copies, waits for them, and re-layouts, per_device(): placed.reshape(lax.axis_size('vis') * panel_rows, chan_count, 2, grid_width)  23.6 us
    reshape x1, local copies, waits for them, and re-layouts, per_device(): shard_rows.reshape(rows_here, chan_count, 2, tiles_count, tile_width)  15.8 us
    dot_general x1, matrix products, per_device(): jnp.einsum('omir,rcikn->cokmn', kernel_rows, picked, preferred_element_ty...  15.2 us
    unnamed x15, local copies, waits for them, and re-layouts  14.4 us
    convert_element_type x1, local copies, waits for them, and re-layouts, per_device(): partial_tiles = jnp.einsum('omir,cokmn->rcikn', kernel_rows, residual, pr...  7.97 us
    dot_general x1, matrix products, per_device(): jnp.einsum('rcikn,kt->rcitn', partial_tiles, one_hot, preferred_element_t...  7.84 us
  transfers between devices with their start and end apart: 4, of which 4 were waited for; matrix products, arithmetic and copies ran while one was open for 4% of the time, Pallas kernels for 0%

profile of v1, /device:TPU:1, one launch (start us, length us, event | category | flops | bytes accessed | tf_op | source)
XLA Modules:
  0.0 327.5 jit_solution(2221733193606426772)
XLA Ops:
  7.2 0.1 broadcast_multiply_fusion
  7.3 0.4 fusion.58
  7.7 1.4 reshape_reshape.3
  9.1 0.7 fusion.97
  9.8 0.4 fusion.20
  10.2 0.8 subtract_bitcast_fusion.1
  11.0 1.1 fusion.54
  12.1 1.1 fusion.50
  13.2 1.1 fusion.24
  14.3 0.5 copy.80
  14.8 1.0 mul.458
  15.8 1.1 fusion.23
  16.9 0.5 copy.83
  17.5 1.0 mul.462
  18.5 1.2 pad_maximum_fusion.2
  19.7 0.2 all-reduce.3.cloned.1.call-start
  19.9 11.4 %copy.86 = bf16[1,1,4,2,16,256,128]{5,6,4,3,2,1,0:T(8,128)(2,1)} copy(bf16[1,1,4,2,16,256,128]{6,5,4,3,2,1,0:T(8,128)(2,1)} %param.11) | data formatting | bytes 16777216 | tf_op args[4]
  32.1 47.8 %all-gather.3.cloned.1.call-done = bf16[128,4,2,4096]{3,1,0,2:T(4,128)(2,1)} async-done(((bf16[8,4,2,4096]{3,1,0,2:T(4,128)(2,1)}), bf16[128,4,2,4096]{3,1,0,2:T(4,128)(2,1)}) %all-gather.3.cloned.1.call-update) | async-done | bytes 8388624 | tf_op jit(solution)/shard_map/all_gather | solution.py:103
  80.0 15.8 %reshape.137 = bf16[128,4,2,32,128]{4,3,1,0,2:T(8,128)(2,1)} reshape(bf16[128,4,2,4096]{3,1,0,2:T(4,128)(2,1)} %all-gather.3.cloned.1.call-done) | data formatting | bytes 16777216 | tf_op jit(solution)/shard_map/reshape | solution.py:105
  95.7 4.7 %convert_bitcast_fusion.1 = bf16[128,4,2,16,128,1]{4,3,2,1,0,5:T(8,128)(2,1)S(1)} fusion(bf16[128,4,2,32,128]{4,3,1,0,2:T(8,128)(2,1)} %reshape.137, s32[16]{0:T(128)S(1)} %bitcast.131), kind=kOutput, calls=%fused_computation.12 | convolution fusion | flops 136315392 | bytes 12582976 | tf_op jit(solution)/shard_map/rcitn,kt->rcikn/dot_general | solution.py:106
  100.4 15.2 %fusion.6 = bf16[4,2,16,256,128,1]{3,4,2,1,0,5:T(8,128)(2,1)} fusion(bf16[1,1,4,2,16,256,128]{5,6,4,3,2,1,0:T(8,128)(2,1)} %copy.86, pred[16]{0:T(512)(128)(4,1)S(1)} %iota_compare_fusion.1, bf16[128,4,2,16,128,1]{4,3,2,1,0,5:T(8,128)(2,1)S(1)} %convert_bitcast_fusion.1, bf16[1,256,2,128]{3,1,2,0:T(8,128)(2,1)S(1)} %get-tuple-element.15, ...), kind=kOutput, calls=%fused_computation.9 | convolution fusion | flops 2164785152 | bytes 21233680 | tf_op jit(solution)/shard_map/omir,rcikn->cokmn/dot_general | solution.py:110
  115.6 7.7 %fusion.7 = bf16[128,4,2,16,128]{0,4,2,3,1:T(8,128)(2,1)} fusion(bf16[4,2,16,256,128,1]{3,4,2,1,0,5:T(8,128)(2,1)} %fusion.6, bf16[1,256,2,128]{3,1,2,0:T(8,128)(2,1)S(1)} %get-tuple-element.15, bf16[1,256,2,128]{3,1,2,0:T(8,128)(2,1)S(1)} %get-tuple-element.14), kind=kOutput, calls=%fused_computation.10 | convolution fusion | flops 2149711872 | bytes 12845056 | tf_op jit(solution)/shard_map/omir,cokmn->rcikn/dot_general | solution.py:117
  123.3 8.0 %copy.89 = bf16[128,4,2,16,128]{4,3,2,1,0:T(8,128)(2,1)} copy(bf16[128,4,2,16,128]{0,4,2,3,1:T(8,128)(2,1)} %fusion.7) | data formatting | bytes 8388608 | tf_op jit(solution)/shard_map/convert_element_type | solution.py:119
  131.3 7.8 %convert_bitcast_fusion = bf16[128,4,2,32,128]{4,3,2,1,0:T(8,128)(2,1)} fusion(bf16[128,4,2,16,128]{4,3,2,1,0:T(8,128)(2,1)} %copy.89, s32[16]{0:T(128)S(1)} %bitcast.132), kind=kOutput, calls=%fused_computation.8 | convolution fusion | flops 138412544 | bytes 12582976 | tf_op jit(solution)/shard_map/rcikn,kt->rcitn/dot_general | solution.py:120
  139.2 12.5 %convert_element_type.128 = bf16[128,4,2,4096]{3,2,1,0:T(2,128)(2,1)} reshape(bf16[128,4,2,32,128]{4,3,2,1,0:T(8,128)(2,1)} %convert_bitcast_fusion) | data formatting | bytes 16777216 | tf_op jit(solution)/shard_map/convert_element_type | solution.py:124
  151.7 11.0 %copy.90 = bf16[128,4,2,4096]{3,1,2,0:T(4,128)(2,1)} copy(bf16[128,4,2,4096]{3,2,1,0:T(2,128)(2,1)} %convert_element_type.128) | data formatting | bytes 16777216 | tf_op jit(solution)/shard_map/convert_element_type | solution.py:124
  162.8 1.0 copy-done
  163.8 1.9 collective-permute-start
  165.8 0.6 dynamic-slice
  167.1 0.3 collective-permute-done
  167.4 127.4 %all-reduce.3.cloned.1.call-done = bf16[128,4,2,4096]{3,1,2,0:T(4,128)(2,1)} async-done(((bf16[128,4,2,4096]{3,1,2,0:T(4,128)(2,1)}), bf16[128,4,2,4096]{3,1,2,0:T(4,128)(2,1)}) %all-reduce.3.cloned.1.call-update) | async-done | bytes 8388624
  294.7 1.2 constant_dynamic-slice_fusion
  296.0 0.5 copy.91
  296.5 2.3 slice_reduce_fusion.1
  298.8 0.4 fusion.92
  299.3 0.4 fusion.94
  299.8 0.4 convolution_add_fusion
  300.2 0.6 add_bitcast_fusion
  300.8 1.1 fusion.47
  301.9 1.1 fusion.14
  302.9 0.6 copy.94
  303.6 0.9 mul.470
  304.5 2.4 multiply_subtract_fusion
  307.0 4.0 %collective-permute-start.1 = (bf16[3,4,4096]{2,1,0:T(4,128)(2,1)S(1)}, bf16[3,4,4096]{2,1,0:T(4,128)(2,1)S(1)}, u32[]{:S(2)}, u32[]{:S(2)}) collective-permute-start(bf16[3,4,4096]{2,1,0:T(4,128)(2,1)S(1)} %slice.138), channel_id=1, source_target_pairs={{2,0},{4,2},{6,4},{8,6},{10,8},{12,10},{14,12},{16,14},{18,16},{20... | collective-permute-start | bytes 294920 | tf_op jit(solution)/shard_map/ppermute | solution.py:25
  311.0 1.9 collective-permute-done.1
  312.9 0.7 multiply_reduce_fusion
  313.6 6.0 %all-gather = bf16[16,4096]{1,0:T(8,128)(2,1)S(1)} all-gather(bf16[8,4096]{1,0:T(8,128)(2,1)S(1)} %get-tuple-element.4), channel_id=2, replica_groups=mesh['facet'=8,'vis'=16,'spec'=2] {'spec'}, dimensions={0}, use_global_device_ids=true | all-gather | bytes 196608 | tf_op jit(solution)/shard_map/all_gather | solution.py:152
  319.7 1.0 multiply_divide_fusion
  (25 shorter events, 0.5 us)
Async XLA Ops:
  7.2 72.8 %all-gather.3.cloned.1.call-start = ((), (), s32[]{:S(2)}) async-start(), calls=%async_computation | async-start | bytes 8912896 | tf_op jit(solution)/shard_map/all_gather | solution.py:103
  19.7 12.4 %copy-start.2 = (bf16[1,1,2,256,128]{4,3,2,1,0:T(8,128)(2,1)S(1)}, bf16[1,1,2,256,128]{4,3,2,1,0:T(8,128)(2,1)}, u32[]{:S(2)}) copy-start(bf16[1,1,2,256,128]{4,3,2,1,0:T(8,128)(2,1)} %param.10) | copy-start | bytes 393220
  19.7 275.0 %all-reduce.3.cloned.1.call-start = ((), (), s32[]{:S(2)}) async-start(), calls=%async_computation.1 | async-start | bytes 16777216
  32.1 63.6 %copy-start.3 = (s32[1,1,16]{2,1,0:T(1,128)S(1)}, s32[1,1,16]{2,1,0:T(1,128)}, u32[]{:S(2)}) copy-start(s32[1,1,16]{2,1,0:T(1,128)} %param.12) | copy-start | bytes 196
  162.7 1.0 copy-start
  162.7 3.0 copy-start.4
  163.8 3.5 %collective-permute-start = (bf16[3,4,4096]{2,1,0:T(4,128)(2,1)S(1)}, bf16[3,4,4096]{2,1,0:T(4,128)(2,1)S(1)}, u32[]{:S(2)}, u32[]{:S(2)}) collective-permute-start(bf16[3,4,4096]{2,1,0:T(4,128)(2,1)S(1)} %slice.139), channel_id=1, source_target_pairs={{0,2},{2,4},{4,6},{6,8},{8,10},{10,12},{12,14},{14,16},{16,18},{18... | collective-permute-start | bytes 294920 | tf_op jit(solution)/shard_map/ppermute | solution.py:25
  299.7 19.9 %copy-start.1 = (f32[8,4096]{1,0:T(8,128)S(1)}, f32[8,4096]{1,0:T(8,128)}, u32[]{:S(2)}) copy-start(f32[8,4096]{1,0:T(8,128)} %param.9) | copy-start | bytes 393220
  307.0 5.9 %collective-permute-start.1 = (bf16[3,4,4096]{2,1,0:T(4,128)(2,1)S(1)}, bf16[3,4,4096]{2,1,0:T(4,128)(2,1)S(1)}, u32[]{:S(2)}, u32[]{:S(2)}) collective-permute-start(bf16[3,4,4096]{2,1,0:T(4,128)(2,1)S(1)} %slice.138), channel_id=1, source_target_pairs={{2,0},{4,2},{6,4},{8,6},{10,8},{12,10},{14,12},{16,14},{18,16},{20... | collective-permute-start | bytes 294920 | tf_op jit(solution)/shard_map/ppermute | solution.py:25
Sparse Core Ops, SparseCore 0:
  19.8 60.1 all-gather.2
  162.9 131.8 all-reduce.2
